TPU v7x, 32 devices: a whole 2x2x4 slice. The times are simulated.
32 devices in a mesh: row: 8 (over z, core), col: 4 (over y, x).
Axes of the slice: x: 2, y: 2, z: 4, core: 2. Of those that a mesh axis runs over, the one named last changes fastest.
Arguments:
- trunk_in: bfloat16 [1536, 8192], P('col', 'row'), may hold values from -24 to 24
- conv_weight: bfloat16 [5, 1536, 1536], P(None, 'col'), may hold values from -0.0625 to 0.0625
- conv_bias: float32 [1536], P('col'), may hold values from -3 to 3
- norm_gain: float32 [1536], replicated, may hold values from 0.1 to 1.9
- pair_proj: bfloat16 [64, 1536], replicated, may hold values from -0.15625 to 0.15625
- pair_in: bfloat16 [512, 128, 128], P('row', 'col'), may hold values from -6 to 6
- opm_weight: bfloat16 [1024, 128], replicated, may hold values from -0.1875 to 0.1875
- pair_bias: float32 [128], replicated, may hold values from -3 to 3
Outputs:
- trunk_out: bfloat16 [1536, 8192], P('col', 'row')
- pair_out: bfloat16 [512, 128, 128], P('row', 'col')
All inputs are finite; a program needn't handle non-finite values.
Results may differ from a plain program's by a relative error of at most 0.012.
Values may be sent and summed in bfloat16 or wider, within the bound.
No kernel may reach another device: no remote copies, remote signals or barrier semaphores. Data moves between devices by JAX's collectives and lax.ppermute only.
A program may use at most 64 MiB of HBM per device.

v0:
```python
import jax
import jax.numpy as jnp
from jax import lax
from jax.sharding import PartitionSpec as P

TRUNK_CHANNELS = 1536
DILATION_STEP = 8
POOL = 16
OPM = 32
WINDOWS = 4
EPSILON = 1e-05


def with_halo(cells, sides, width):
    for axis, dim in sides:
        count = lax.axis_size(axis)
        ends = count - 1
        head = lax.slice_in_dim(cells, 0, width, axis=dim)
        tail = lax.slice_in_dim(cells, cells.shape[dim] - width, cells.shape[dim], axis=dim)
        cells = jnp.concatenate(
            [
                lax.ppermute(tail, axis, [(i, (i + 1) % count) for i in range(ends)]),
                cells,
                lax.ppermute(head, axis, [((i + 1) % count, i) for i in range(ends)]),
            ],
            axis=dim,
        )
    return cells


def partner_2(block, axis, bit):
    count = lax.axis_size(axis)
    route = []
    for low in range(count):
        high = low | 1 << bit
        if high != low and high < count:
            route += [(low, high), (high, low)]
    return lax.ppermute(block, axis, route)


def per_device(
    trunk_in, conv_weight, conv_bias, norm_gain, pair_proj, pair_in, opm_weight, pair_bias
):
    local_channels = trunk_in.shape[0]
    token_positions = trunk_in.shape[1]
    kernel = conv_weight.shape[0]
    border_width = 2 * DILATION_STEP
    per_window = lax.axis_size("row") // WINDOWS
    row_index = lax.axis_index("row")
    col_index = lax.axis_index("col")
    in_window = row_index % per_window
    source = trunk_in.astype(jnp.float32)
    zero_sum = jnp.zeros((local_channels, token_positions), jnp.float32)
    squares = lax.psum(jnp.sum(source * source, axis=0), "col")
    scale = lax.rsqrt(squares / TRUNK_CHANNELS + EPSILON)[None, :]
    own_gain = lax.dynamic_slice_in_dim(norm_gain, col_index * local_channels, local_channels, 0)
    gelu_output = jax.nn.gelu(source * own_gain[:, None] * scale).astype(jnp.bfloat16)
    padded_trunk = with_halo(gelu_output, (("row", 1),), border_width)
    carried = zero_sum
    piece = lax.all_gather(padded_trunk, "col", axis=0, tiled=True)
    for tap_offset in range(kernel):
        carried = carried + jnp.dot(
            conv_weight[tap_offset],
            piece[:, tap_offset * DILATION_STEP : tap_offset * DILATION_STEP + token_positions],
            preferred_element_type=jnp.float32,
        )
    trunk_out = (source + carried + conv_bias[:, None]).astype(jnp.bfloat16)
    pooled = (
        trunk_out.astype(jnp.float32)
        .reshape(local_channels, token_positions // POOL, POOL)
        .mean(axis=2)
        .astype(jnp.bfloat16)
    )
    own_proj = lax.dynamic_slice_in_dim(pair_proj, col_index * local_channels, local_channels, 1)
    pooled_f = pooled.astype(jnp.float32)
    partial_proj = lax.dot_general(
        pooled, own_proj, (((0,), (1,)), ((), ())), preferred_element_type=jnp.float32
    )
    projected, sums = lax.psum((partial_proj, jnp.sum(pooled_f * pooled_f, axis=0)), "col")
    sides = (projected * lax.rsqrt(sums / TRUNK_CHANNELS + EPSILON)[:, None]).astype(jnp.bfloat16)
    row_side = sides[:, :OPM]
    collected = sides[:, OPM:]
    col_block = pair_in.shape[1]
    pooled_rows = row_side.shape[0]
    for bit_num in range(per_window.bit_length() - 1):
        partner = partner_2(collected, "row", bit_num)
        upper_half = in_window // 2**bit_num % 2 == 1
        collected = jnp.where(
            upper_half,
            jnp.concatenate([partner, collected], axis=0),
            jnp.concatenate([collected, partner], axis=0),
        )
    own_cols = lax.dynamic_slice_in_dim(collected, col_index * col_block, col_block, 0)
    outer = (
        row_side.astype(jnp.float32)[:, None, :, None]
        * own_cols.astype(jnp.float32)[None, :, None, :]
    ).astype(jnp.bfloat16)
    outer = outer.reshape(pooled_rows * col_block, OPM * OPM)
    update = jnp.dot(outer, opm_weight, preferred_element_type=jnp.float32).reshape(pair_in.shape)
    pair_out = (pair_in.astype(jnp.float32) + update + pair_bias).astype(jnp.bfloat16)
    return (trunk_out, pair_out)


def solution(mesh):
    return jax.shard_map(
        per_device,
        mesh=mesh,
        in_specs=(
            P("col", "row"),
            P(None, "col", None),
            P("col"),
            P(),
            P(),
            P("row", "col", None),
            P(),
            P(),
        ),
        out_specs=(P("col", "row"), P("row", "col", None)),
        check_vma=False,
    )
```

profile of v0, /device:TPU:0, one launch (start us, length us, event | category | flops | bytes accessed | tf_op | source)
XLA Modules:
  0.0 115.7 jit_solution(4807338806114271744)
XLA Ops:
  7.2 0.0 copy-start
  7.2 0.0 all-gather.2.cloned.1.call-start
  7.2 1.5 %copy.25 = bf16[384,1024]{0,1:T(8,128)(2,1)S(1)} copy(bf16[384,1024]{1,0:T(8,128)(2,1)} %param.8) | data formatting | bytes 1572864 | tf_op args[0]
  8.8 0.2 fusion.21
  9.0 11.4 %psum.21 = f32[1024]{0:T(1024)S(1)} all-reduce(f32[1024]{0:T(1024)S(1)} %fusion.21), channel_id=1, replica_groups=mesh['row'=8,'col'=4] {'col'}, use_global_device_ids=true, to_apply=%region_1.2 | all-reduce | flops 1024 | bytes 8192 | tf_op jit(solution)/shard_map/psum | solution.py:54
  20.4 0.8 dynamic_slice.9
  21.2 0.7 fusion.16
  21.9 1.3 %collective-permute-start = (bf16[384,16]{0,1:T(8,128)(2,1)S(1)}, bf16[384,16]{0,1:T(8,128)(2,1)S(1)}, u32[]{:S(2)}, u32[]{:S(2)}) collective-permute-start(bf16[384,16]{0,1:T(8,128)(2,1)S(1)} %get-tuple-element.12), channel_id=1, source_target_pairs={{0,4},{4,8},{8,12},{12,16},{16,20},{20,24},{24,28},{1,5},{5,9},{9,... | collective-permute-start | bytes 36872 | tf_op jit(solution)/shard_map/ppermute | solution.py:22
  23.2 1.3 %collective-permute-start.1 = (bf16[384,16]{0,1:T(8,128)(2,1)S(1)}, bf16[384,16]{0,1:T(8,128)(2,1)S(1)}, u32[]{:S(2)}, u32[]{:S(2)}) collective-permute-start(bf16[384,16]{0,1:T(8,128)(2,1)S(1)} %get-tuple-element.13), channel_id=1, source_target_pairs={{4,0},{8,4},{12,8},{16,12},{20,16},{24,20},{28,24},{5,1},{9,5},{13... | collective-permute-start | bytes 36872 | tf_op jit(solution)/shard_map/ppermute | solution.py:24
  24.5 3.6 %collective-permute-done.1 = bf16[384,16]{0,1:T(8,128)(2,1)S(1)} collective-permute-done((bf16[384,16]{0,1:T(8,128)(2,1)S(1)}, bf16[384,16]{0,1:T(8,128)(2,1)S(1)}, u32[]{:S(2)}, u32[]{:S(2)}) %collective-permute-start.1) | collective-permute-done | bytes 12320 | tf_op jit(solution)/shard_map/ppermute | solution.py:24
  28.1 1.0 pad_maximum_fusion
  29.1 0.0 all-gather.2.cloned.1.call-update
  29.1 45.1 %all-gather.2.cloned.1.call-done = bf16[1536,1056]{0,1:T(8,128)(2,1)} async-done(((bf16[384,1056]{0,1:T(8,128)(2,1)}), bf16[1536,1056]{0,1:T(8,128)(2,1)}) %all-gather.2.cloned.1.call-update) | async-done | bytes 3244048 | tf_op jit(solution)/shard_map/all_gather | solution.py:60
  74.2 4.2 %fusion.5 = f32[1024,384]{1,0:T(8,128)S(1)} fusion(bf16[1536,1056]{0,1:T(8,128)(2,1)} %all-gather.2.cloned.1.call-done, bf16[5,384,1536]{2,1,0:T(8,128)(2,1)} %param.9), kind=kOutput, calls=%fused_computation.6 | convolution fusion | flops 1207959552 | bytes 5898240 | tf_op jit(solution)/shard_map/dot_general | solution.py:62
  78.4 0.0 slice-start.1
  78.4 3.2 %fusion.7 = f32[1024,384]{1,0:T(8,128)S(1)} fusion(bf16[1536,1056]{0,1:T(8,128)(2,1)S(1)} %copy-done.1, bf16[5,384,1536]{2,1,0:T(8,128)(2,1)} %param.9), kind=kOutput, calls=%fused_computation.8 | convolution fusion | flops 1207959552 | bytes 5898240 | tf_op jit(solution)/shard_map/dot_general | solution.py:62
  81.6 1.8 %fusion.9 = f32[1024,384]{1,0:T(8,128)S(1)} fusion(bf16[1536,1056]{0,1:T(8,128)(2,1)S(1)} %copy-done.1, bf16[5,384,1536]{2,1,0:T(8,128)(2,1)S(1)} %bitcast.28), kind=kOutput, calls=%fused_computation.10 | convolution fusion | flops 1207959552 | bytes 5898240 | tf_op jit(solution)/shard_map/dot_general | solution.py:62
  83.4 0.0 copy-start.3
  83.5 1.8 %fusion.11 = f32[1024,384]{1,0:T(8,128)S(1)} fusion(bf16[1536,1056]{0,1:T(8,128)(2,1)S(1)} %copy-done.1, bf16[5,384,1536]{2,1,0:T(8,128)(2,1)S(1)} %bitcast.28), kind=kOutput, calls=%fused_computation.12 | convolution fusion | flops 1207959552 | bytes 5898240 | tf_op jit(solution)/shard_map/dot_general | solution.py:62
  85.3 2.2 %convert_reduce_fusion = (f32[384,64]{0,1:T(8,128)S(1)}, bf16[384,1024]{0,1:T(8,128)(2,1)S(1)}) fusion(f32[384]{0:T(512)S(1)} %copy-done.3, bf16[5,384,1536]{2,1,0:T(8,128)(2,1)S(1)} %bitcast.28, bf16[1536,1056]{0,1:T(8,128)(2,1)S(1)} %copy-done.1, f32[1024,384]{1,0:T(8,128)S(1)} %fusion.5, f32[1024,384]{1,0:T(8,128)S(1)} %fusion.7, ...), kind=kOutput, calls=%fused_computation.30 | convolution fusion | flops 1211867136 | bytes 12290048 | tf_op jit(solution)/shard_map/dot_general | solution.py:62
  87.5 0.1 multiply_reduce_fusion
  87.6 0.9 fusion.41
  88.6 15.8 %all-reduce = (f32[64,64]{0,1:T(8,128)S(1)}, f32[64]{0:T(128)S(1)}) all-reduce(f32[64,64]{0,1:T(8,128)S(1)} %fusion.41, f32[64]{0:T(128)S(1)} %multiply_reduce_fusion), channel_id=1, replica_groups=mesh['row'=8,'col'=4] {'col'}, use_global_device_ids=true, to_apply=%region_3.4 | all-reduce | flops 4160 | bytes 33280 | tf_op jit(solution)/shard_map/psum | solution.py:79
  104.4 0.1 collective-permute-start.2
  104.5 1.2 %copy.29 = bf16[384,1024]{1,0:T(8,128)(2,1)} copy(bf16[384,1024]{0,1:T(8,128)(2,1)S(1)} %get-tuple-element.17) | data formatting | bytes 1572864
  105.8 0.2 copy.27
  105.9 0.0 collective-permute-done.2
  106.0 0.1 fusion.44
  106.1 0.1 copy.28
  106.2 0.2 mul.102
  106.4 0.3 copy-done.2
  106.8 2.1 %fusion.29 = bf16[64,32,128]{2,1,0:T(8,128)(2,1)} fusion(f32[32,1024]{1,0:T(8,128)S(1)} %mul.102, f32[64,1024]{1,0:T(8,128)S(1)} %copy.27, bf16[64,32,128]{2,1,0:T(8,128)(2,1)S(1)} %copy-done.2, f32[128]{0:T(128)S(1)} %copy-done.4, bf16[1024,128]{1,0:T(8,128)(2,1)S(1)} %copy-done), kind=kOutput, calls=%fused_computation.33 | convolution fusion | flops 542113792 | bytes 1704448 | tf_op jit(solution)/shard_map/dot_general | solution.py:99
  (19 shorter events, 0.1 us)
Async XLA Ops:
  7.2 99.3 %copy-start = (bf16[1024,128]{1,0:T(8,128)(2,1)S(1)}, bf16[1024,128]{1,0:T(8,128)(2,1)}, u32[]{:S(2)}) copy-start(bf16[1024,128]{1,0:T(8,128)(2,1)} %param.14) | copy-start | bytes 786436
  7.2 67.0 %all-gather.2.cloned.1.call-start = ((), (), s32[]{:S(2)}) async-start(), calls=%async_computation | async-start | bytes 4055040 | tf_op jit(solution)/shard_map/all_gather | solution.py:60
  21.9 2.6 %collective-permute-start = (bf16[384,16]{0,1:T(8,128)(2,1)S(1)}, bf16[384,16]{0,1:T(8,128)(2,1)S(1)}, u32[]{:S(2)}, u32[]{:S(2)}) collective-permute-start(bf16[384,16]{0,1:T(8,128)(2,1)S(1)} %get-tuple-element.12), channel_id=1, source_target_pairs={{0,4},{4,8},{8,12},{12,16},{16,20},{20,24},{24,28},{1,5},{5,9},{9,... | collective-permute-start | bytes 36872 | tf_op jit(solution)/shard_map/ppermute | solution.py:22
  23.2 4.9 %collective-permute-start.1 = (bf16[384,16]{0,1:T(8,128)(2,1)S(1)}, bf16[384,16]{0,1:T(8,128)(2,1)S(1)}, u32[]{:S(2)}, u32[]{:S(2)}) collective-permute-start(bf16[384,16]{0,1:T(8,128)(2,1)S(1)} %get-tuple-element.13), channel_id=1, source_target_pairs={{4,0},{8,4},{12,8},{16,12},{20,16},{24,20},{28,24},{5,1},{9,5},{13... | collective-permute-start | bytes 36872 | tf_op jit(solution)/shard_map/ppermute | solution.py:24
  74.2 4.2 %copy-start.1 = (bf16[1536,1056]{0,1:T(8,128)(2,1)S(1)}, bf16[1536,1056]{0,1:T(8,128)(2,1)}, u32[]{:S(2)}) copy-start(bf16[1536,1056]{0,1:T(8,128)(2,1)} %all-gather.2.cloned.1.call-done) | copy-start | bytes 9732100
  74.2 7.4 %slice-start = ((s8[5898240]{0:T(1024)(128)(4,1)}), s8[4194304]{0:T(1024)(128)(4,1)S(1)}, s32[]{:S(2)}) async-start(s8[5898240]{0:T(1024)(128)(4,1)} %bitcast.27), calls=%async_computation.1 | async-start | bytes 8388608
  78.4 3.2 %slice-start.1 = ((s8[5898240]{0:T(1024)(128)(4,1)}), s8[1703936]{0:T(1024)(128)(4,1)S(1)}, s32[]{:S(2)}) async-start(s8[5898240]{0:T(1024)(128)(4,1)} %bitcast.27), calls=%async_computation.2 | async-start | bytes 3407872
  83.4 1.8 %copy-start.3 = (f32[384]{0:T(512)S(1)}, f32[384]{0:T(512)}, u32[]{:S(2)}) copy-start(f32[384]{0:T(512)} %param.10) | copy-start | bytes 4612
  104.4 1.5 %collective-permute-start.2 = (bf16[64,32]{0,1:T(8,128)(2,1)S(1)}, bf16[64,32]{0,1:T(8,128)(2,1)S(1)}, u32[]{:S(2)}, u32[]{:S(2)}) collective-permute-start(bf16[64,32]{0,1:T(8,128)(2,1)S(1)} %get-tuple-element.15), channel_id=1, source_target_pairs={{0,4},{4,0},{8,12},{12,8},{16,20},{20,16},{24,28},{28,24},{1,5},{5... | collective-permute-start | bytes 12296 | tf_op jit(solution)/shard_map/ppermute | solution.py:38
  105.7 1.0 copy-start.2
  105.7 1.0 copy-start.4
Sparse Core Ops, SparseCore 0:
  29.2 44.9 all-gather.1
where the time goes:
time: 116 us
  waiting for transfers between devices  48.7 us (42%)
  blocking collectives  27.2 us (23%)
  matrix products  16.2 us (14%)
  between operations  14.3 us (12%)
  local copies, waits for them, and re-layouts  4.39 us (4%)
  starting transfers between devices  2.69 us (2%)
  other arithmetic  2.16 us (2%)
    all_gather x1, waiting for transfers between devices, per_device(): piece = lax.all_gather(padded_trunk, 'col', axis=0, tiled=True)  45.1 us
    psum x1, blocking collectives, per_device(): lax.psum((partial_proj, jnp.sum(pooled_f * pooled_f, axis=0)), 'col')  15.8 us
    dot_general x5, matrix products, per_device(): jnp.dot(conv_weight[tap_offset], piece[:, tap_offset * DILATION_STEP:tap_...  13.2 us
    psum x1, blocking collectives, per_device(): squares = lax.psum(jnp.sum(source * source, axis=0), 'col')  11.4 us
    ppermute x1, waiting for transfers between devices, with_halo(): lax.ppermute(head, axis, [((i + 1) % count, i) for i in range(ends)])  3.57 us
    unnamed x16, local copies, waits for them, and re-layouts  3.06 us
  transfers between devices with their start and end apart: 4, of which 2 were waited for; matrix products, arithmetic and copies ran while one was open for 1% of the time, Pallas kernels for 0%

commit v1 on v0

--- a/solution.py
+++ b/solution.py
@@ -57,7 +57,16 @@
     gelu_output = jax.nn.gelu(source * own_gain[:, None] * scale).astype(jnp.bfloat16)
     padded_trunk = with_halo(gelu_output, (("row", 1),), border_width)
     carried = zero_sum
-    piece = lax.all_gather(padded_trunk, "col", axis=0, tiled=True)
+    enter_the_members_all = lambda vec: jnp.concatenate(
+        lax.all_to_all(
+            jnp.stack([vec for _ in range(lax.axis_size("col"))], axis=0),
+            "col",
+            split_axis=0,
+            concat_axis=0,
+        ),
+        axis=0,
+    )
+    piece = enter_the_members_all(padded_trunk)
     for tap_offset in range(kernel):
         carried = carried + jnp.dot(
             conv_weight[tap_offset],

time: 116 us -> 93.9 us (0.81)
  waiting for transfers between devices: 48.7 us -> 3.58 us
  blocking collectives: 27.2 us -> 66.9 us
  between operations: 14.3 us -> 0.89 us
  matrix products: 16.2 us -> 12.4 us
    all_gather x1 -> x0, waiting for transfers between devices: 45.1 us -> none  [per_device(): piece = lax.all_gather(padded_trunk, 'col', axis=0, tiled=True)]
    all_to_all x0 -> x1, blocking collectives: none -> 40.3 us  [per_device(): lax.all_to_all(jnp.stack([vec for _ in range(lax.axis_size('col'))], axis...]
    dot_general x5, matrix products: 13.2 us -> 9.43 us  [per_device(): jnp.dot(conv_weight[tap_offset], piece[:, tap_offset * DILATION_STEP:tap_...]
    unnamed x16 -> x14, local copies, waits for them, and re-layouts: 3.06 us -> 3.06 us
  transfers between devices with their start and end apart: 4 -> 3, of which waited for: 2 -> 1; matrix products, arithmetic and copies ran while one was open for 1% -> 1% of each run, Pallas kernels for 0% -> 0%
where the time goes in v1:
time: 93.9 us; the launch traced here: 92.8 us
  blocking collectives  66.9 us (71%)
  matrix products  12.4 us (13%)
  local copies, waits for them, and re-layouts  5.03 us (5%)
  waiting for transfers between devices  3.58 us (4%)
  starting transfers between devices  2.65 us (3%)
  other arithmetic  1.25 us (1%)
    all_to_all x1, blocking collectives, per_device(): lax.all_to_all(jnp.stack([vec for _ in range(lax.axis_size('col'))], axis...  40.3 us
    psum x1, blocking collectives, per_device(): lax.psum((partial_proj, jnp.sum(pooled_f * pooled_f, axis=0)), 'col')  15.2 us
    psum x1, blocking collectives, per_device(): squares = lax.psum(jnp.sum(source * source, axis=0), 'col')  11.4 us
    dot_general x5, matrix products, per_device(): jnp.dot(conv_weight[tap_offset], piece[:, tap_offset * DILATION_STEP:tap_...  9.43 us
    ppermute x1, waiting for transfers between devices, with_halo(): lax.ppermute(head, axis, [((i + 1) % count, i) for i in range(ends)])  3.57 us
    unnamed x14, local copies, waits for them, and re-layouts  3.06 us
    dot_general x1, matrix products, per_device(): jnp.dot(outer, opm_weight, preferred_element_type=jnp.float32)  2.05 us
  transfers between devices with their start and end apart: 3, of which 1 were waited for; matrix products, arithmetic and copies ran while one was open for 1% of the time, Pallas kernels for 0%

profile of v1, /device:TPU:0, one launch (start us, length us, event | category | flops | bytes accessed | tf_op | source)
XLA Modules:
  0.0 92.8 jit_solution(13858245376016779937)
XLA Ops:
  0.6 0.0 copy-start
  0.7 1.5 %copy.37 = bf16[384,1024]{0,1:T(8,128)(2,1)S(1)} copy(bf16[384,1024]{1,0:T(8,128)(2,1)} %param.8) | data formatting | bytes 1572864 | tf_op args[0]
  2.2 0.2 fusion.21
  2.4 11.4 %psum.21 = f32[1024]{0:T(1024)S(1)} all-reduce(f32[1024]{0:T(1024)S(1)} %fusion.21), channel_id=1, replica_groups=mesh['row'=8,'col'=4] {'col'}, use_global_device_ids=true, to_apply=%region_1.2 | all-reduce | flops 1024 | bytes 8192 | tf_op jit(solution)/shard_map/psum | solution.py:54
  13.8 0.8 dynamic_slice.9
  14.6 0.7 fusion.16
  15.3 1.3 %collective-permute-start = (bf16[384,16]{0,1:T(8,128)(2,1)S(1)}, bf16[384,16]{0,1:T(8,128)(2,1)S(1)}, u32[]{:S(2)}, u32[]{:S(2)}) collective-permute-start(bf16[384,16]{0,1:T(8,128)(2,1)S(1)} %get-tuple-element.14), channel_id=1, source_target_pairs={{0,4},{4,8},{8,12},{12,16},{16,20},{20,24},{24,28},{1,5},{5,9},{9,... | collective-permute-start | bytes 36872 | tf_op jit(solution)/shard_map/ppermute | solution.py:22
  16.6 1.3 %collective-permute-start.1 = (bf16[384,16]{0,1:T(8,128)(2,1)S(1)}, bf16[384,16]{0,1:T(8,128)(2,1)S(1)}, u32[]{:S(2)}, u32[]{:S(2)}) collective-permute-start(bf16[384,16]{0,1:T(8,128)(2,1)S(1)} %get-tuple-element.15), channel_id=1, source_target_pairs={{4,0},{8,4},{12,8},{16,12},{20,16},{24,20},{28,24},{5,1},{9,5},{13... | collective-permute-start | bytes 36872 | tf_op jit(solution)/shard_map/ppermute | solution.py:24
  17.9 3.6 %collective-permute-done.1 = bf16[384,16]{0,1:T(8,128)(2,1)S(1)} collective-permute-done((bf16[384,16]{0,1:T(8,128)(2,1)S(1)}, bf16[384,16]{0,1:T(8,128)(2,1)S(1)}, u32[]{:S(2)}, u32[]{:S(2)}) %collective-permute-start.1) | collective-permute-done | bytes 12320 | tf_op jit(solution)/shard_map/ppermute | solution.py:24
  21.5 0.1 pad_maximum_fusion
  21.6 0.0 slice-start
  21.6 0.3 stack.2
  21.9 0.0 slice-start.1
  21.9 40.3 %all_to_all.5 = bf16[4,384,1056]{1,2,0:T(8,128)(2,1)S(1)} all-to-all(bf16[4,384,1056]{1,2,0:T(8,128)(2,1)S(1)} %stack.2), channel_id=1, replica_groups=mesh['row'=8,'col'=4] {'col'}, dimensions={0} | all-to-all | bytes 6488064 | tf_op jit(solution)/shard_map/all_to_all | solution.py:61
  62.2 0.3 copy.44
  62.6 1.8 %fusion.3 = f32[1024,384]{1,0:T(8,128)S(1)} fusion(bf16[1536,1056]{0,1:T(8,128)(2,1)S(1)} %bitcast.29, bf16[5,384,1536]{2,1,0:T(8,128)(2,1)S(1)} %bitcast.36), kind=kOutput, calls=%fused_computation.4 | convolution fusion | flops 1207959552 | bytes 5898240 | tf_op jit(solution)/shard_map/dot_general | solution.py:71
  64.4 1.8 %fusion.5 = f32[1024,384]{1,0:T(8,128)S(1)} fusion(bf16[1536,1056]{0,1:T(8,128)(2,1)S(1)} %bitcast.30, bf16[5,384,1536]{2,1,0:T(8,128)(2,1)S(1)} %bitcast.36), kind=kOutput, calls=%fused_computation.6 | convolution fusion | flops 1207959552 | bytes 5898240 | tf_op jit(solution)/shard_map/dot_general | solution.py:71
  66.2 1.8 %fusion.7 = f32[1024,384]{1,0:T(8,128)S(1)} fusion(bf16[1536,1056]{0,1:T(8,128)(2,1)S(1)} %bitcast.31, bf16[5,384,1536]{2,1,0:T(8,128)(2,1)S(1)} %bitcast.36), kind=kOutput, calls=%fused_computation.8 | convolution fusion | flops 1207959552 | bytes 5898240 | tf_op jit(solution)/shard_map/dot_general | solution.py:71
  68.0 0.0 copy-start.2
  68.0 1.8 %fusion.9 = f32[1024,384]{1,0:T(8,128)S(1)} fusion(bf16[1536,1056]{0,1:T(8,128)(2,1)S(1)} %bitcast.32, bf16[5,384,1536]{2,1,0:T(8,128)(2,1)S(1)} %bitcast.36), kind=kOutput, calls=%fused_computation.10 | convolution fusion | flops 1207959552 | bytes 5898240 | tf_op jit(solution)/shard_map/dot_general | solution.py:71
  69.8 2.2 %convert_reduce_fusion = (f32[384,64]{0,1:T(8,128)S(1)}, bf16[384,1024]{0,1:T(8,128)(2,1)S(1)}) fusion(f32[384]{0:T(512)S(1)} %copy-done.2, f32[1024,384]{1,0:T(8,128)S(1)} %fusion.3, f32[1024,384]{1,0:T(8,128)S(1)} %fusion.5, f32[1024,384]{1,0:T(8,128)S(1)} %fusion.7, f32[1024,384]{1,0:T(8,128)S(1)} %fusion.9, bf16[5,384,1536]{2,1,0:T(8,128)(2,1)S(1)} %bitcast.36, ...), kind=kOutput, calls=%fused_computation.30 | convolution fusion | flops 1211867136 | bytes 12290048 | tf_op jit(solution)/shard_map/dot_general | solution.py:71
  72.1 0.1 multiply_reduce_fusion
  72.2 0.9 %fusion.41 = f32[64,64]{0,1:T(8,128)S(1)} fusion(bf16[64,1536]{1,0:T(8,128)(2,1)} %param.12, s32[]{:T(128)S(6)} %select_n.28, f32[384,64]{0,1:T(8,128)S(1)} %get-tuple-element.18), kind=kOutput, calls=%fused_computation.48 | convolution fusion | flops 3194880 | bytes 163844 | tf_op jit(solution)/shard_map/dot_general | solution.py:85
  73.1 15.2 %all-reduce = (f32[64,64]{0,1:T(8,128)S(1)}, f32[64]{0:T(128)S(1)}) all-reduce(f32[64,64]{0,1:T(8,128)S(1)} %fusion.41, f32[64]{0:T(128)S(1)} %multiply_reduce_fusion), channel_id=1, replica_groups=mesh['row'=8,'col'=4] {'col'}, use_global_device_ids=true, to_apply=%region_3.4 | all-reduce | flops 4160 | bytes 33280 | tf_op jit(solution)/shard_map/psum | solution.py:88
  88.4 0.1 collective-permute-start.2
  88.5 1.2 %copy.42 = bf16[384,1024]{1,0:T(8,128)(2,1)} copy(bf16[384,1024]{0,1:T(8,128)(2,1)S(1)} %get-tuple-element.19) | data formatting | bytes 1572864
  89.7 0.2 copy.40
  89.9 0.1 fusion.44
  90.0 0.1 copy.41
  90.1 0.2 mul.102
  90.4 0.3 copy-done.1
  90.7 2.1 %fusion.29 = bf16[64,32,128]{2,1,0:T(8,128)(2,1)} fusion(f32[32,1024]{1,0:T(8,128)S(1)} %mul.102, f32[64,1024]{1,0:T(8,128)S(1)} %copy.40, bf16[64,32,128]{2,1,0:T(8,128)(2,1)S(1)} %copy-done.1, f32[128]{0:T(128)S(1)} %copy-done.3, bf16[1024,128]{1,0:T(8,128)(2,1)S(1)} %copy-done), kind=kOutput, calls=%fused_computation.33 | convolution fusion | flops 542113792 | bytes 1704448 | tf_op jit(solution)/shard_map/dot_general | solution.py:108
  (17 shorter events, 0.1 us)
Async XLA Ops:
  0.6 89.7 %copy-start = (bf16[1024,128]{1,0:T(8,128)(2,1)S(1)}, bf16[1024,128]{1,0:T(8,128)(2,1)}, u32[]{:S(2)}) copy-start(bf16[1024,128]{1,0:T(8,128)(2,1)} %param.14) | copy-start | bytes 786436
  15.3 2.6 %collective-permute-start = (bf16[384,16]{0,1:T(8,128)(2,1)S(1)}, bf16[384,16]{0,1:T(8,128)(2,1)S(1)}, u32[]{:S(2)}, u32[]{:S(2)}) collective-permute-start(bf16[384,16]{0,1:T(8,128)(2,1)S(1)} %get-tuple-element.14), channel_id=1, source_target_pairs={{0,4},{4,8},{8,12},{12,16},{16,20},{20,24},{24,28},{1,5},{5,9},{9,... | collective-permute-start | bytes 36872 | tf_op jit(solution)/shard_map/ppermute | solution.py:22
  16.6 4.9 %collective-permute-start.1 = (bf16[384,16]{0,1:T(8,128)(2,1)S(1)}, bf16[384,16]{0,1:T(8,128)(2,1)S(1)}, u32[]{:S(2)}, u32[]{:S(2)}) collective-permute-start(bf16[384,16]{0,1:T(8,128)(2,1)S(1)} %get-tuple-element.15), channel_id=1, source_target_pairs={{4,0},{8,4},{12,8},{16,12},{20,16},{24,20},{28,24},{5,1},{9,5},{13... | collective-permute-start | bytes 36872 | tf_op jit(solution)/shard_map/ppermute | solution.py:24
  21.6 41.0 %slice-start = ((s8[5898240]{0:T(1024)(128)(4,1)}), s8[4194304]{0:T(1024)(128)(4,1)S(1)}, s32[]{:S(2)}) async-start(s8[5898240]{0:T(1024)(128)(4,1)} %bitcast.35), calls=%async_computation.1 | async-start | bytes 8388608
  21.9 40.7 %slice-start.1 = ((s8[5898240]{0:T(1024)(128)(4,1)}), s8[1703936]{0:T(1024)(128)(4,1)S(1)}, s32[]{:S(2)}) async-start(s8[5898240]{0:T(1024)(128)(4,1)} %bitcast.35), calls=%async_computation.2 | async-start | bytes 3407872
  68.0 1.8 %copy-start.2 = (f32[384]{0:T(512)S(1)}, f32[384]{0:T(512)}, u32[]{:S(2)}) copy-start(f32[384]{0:T(512)} %param.10) | copy-start | bytes 4612
  88.4 1.5 %collective-permute-start.2 = (bf16[64,32]{0,1:T(8,128)(2,1)S(1)}, bf16[64,32]{0,1:T(8,128)(2,1)S(1)}, u32[]{:S(2)}, u32[]{:S(2)}) collective-permute-start(bf16[64,32]{0,1:T(8,128)(2,1)S(1)} %get-tuple-element.17), channel_id=1, source_target_pairs={{0,4},{4,0},{8,12},{12,8},{16,20},{20,16},{24,28},{28,24},{1,5},{5... | collective-permute-start | bytes 12296 | tf_op jit(solution)/shard_map/ppermute | solution.py:38
  89.7 1.0 %copy-start.1 = (bf16[64,32,128]{2,1,0:T(8,128)(2,1)S(1)}, bf16[64,32,128]{2,1,0:T(8,128)(2,1)}, u32[]{:S(2)}) copy-start(bf16[64,32,128]{2,1,0:T(8,128)(2,1)} %param.13) | copy-start | bytes 1572868
  89.7 1.0 %copy-start.3 = (f32[128]{0:T(128)S(1)}, f32[128]{0:T(128)}, u32[]{:S(2)}) copy-start(f32[128]{0:T(128)} %param.15) | copy-start | bytes 1540
